TPU v7x, 256 devices: a whole 4x4x8 slice. The times are simulated.
256 devices in a mesh: people: 2 (over x_hi), tm: 64 (over z, y, core), type: 2 (over x_lo).
Axes of the slice: x: 4 (x_hi: 2, x_lo: 2; x = x_hi * 2 + x_lo), y: 4, z: 8, core: 2. Of those that a mesh axis runs over, the one named last changes fastest.
Arguments:
- features: bfloat16 [3, 2, 16384], P(None, 'people', 'tm'), may hold values from -6 to 6
- wear: int32 [2, 16384], P('people', 'tm'), may hold values 0 or 1
- rec_start: int32 [2], P('people'), may hold values from 0 to 255
- rec_end: int32 [2], P('people'), may hold values from 16129 to 16384
- conv_first: bfloat16 [3, 3, 128], replicated, may hold values from -2 to 2
- conv_second: bfloat16 [3, 128, 128], replicated, may hold values from -0.3125 to 0.3125
- emit_weight: bfloat16 [128, 512], P(None, 'type'), may hold values from -0.5 to 0.5
- leave: float32 [8, 64], P('type'), may hold values from 0.002 to 0.5
- jump: float32 [8, 64, 64], P('type'), may hold values from -6 to 6
- init_logits: float32 [8, 64], P('type'), may hold values from -6 to 6
- type_prior: float32 [8], replicated, may hold values from -4 to 4
Outputs:
- loglik_rate: float32 [2, 8], P('people', 'type')
- type_post: float32 [2, 8], P('people', 'type')
- occupancy: float32 [8, 64], P('type')
- filtered: float32 [2, 16384, 8, 64], P('people', 'tm', 'type')
All inputs are finite; a program needn't handle non-finite values. No bound on the sum of `wear` on one device may be relied on, other than what follows from the above.
Results may differ from a plain program's by a relative error of at most 0.0085.
Values may be sent and summed in bfloat16 or wider, within the bound.
No kernel may reach another device: no remote copies, remote signals or barrier semaphores. Data moves between devices by JAX's collectives and lax.ppermute only.
A program may use at most 64 MiB of HBM per device.

v0:
```python
import jax
import jax.numpy as jnp
from jax import lax
from jax.sharding import PartitionSpec as P

HIGH = lax.Precision.HIGHEST


def padded(block, sides, width):
    for axis, dim in sides:
        count = lax.axis_size(axis)
        forward = [(i, i + 1) for i in range(count - 1)]
        backward = [(target, source) for source, target in forward]
        low = lax.ppermute(
            lax.slice_in_dim(block, block.shape[dim] - width, None, axis=dim), axis, forward
        )
        high = lax.ppermute(lax.slice_in_dim(block, 0, width, axis=dim), axis, backward)
        block = jnp.concatenate([low, block, high], axis=dim)
    return block


def prefix(shard, axis, combine, identity):
    size, mine = (lax.axis_size(axis), lax.axis_index(axis))
    everything = jax.tree.map(
        lambda part, kind: lax.all_gather(part.astype(kind), axis),
        shard,
        (jnp.bfloat16, jnp.bfloat16),
    )
    start = jax.tree.map(
        lambda part, zero: jnp.broadcast_to(jnp.asarray(zero, part.dtype), part.shape),
        shard,
        identity,
    )

    def turn(k, before):
        reached = k < mine
        new = combine(
            before, jax.tree.map(lambda part, own: part[k].astype(own.dtype), everything, shard)
        )
        return jax.tree.map(lambda a, b: jnp.where(reached, a, b), new, before)

    return lax.fori_loop(0, size, turn, start)


def chain_join(earlier, later):
    left, left_log = earlier
    right, right_log = later
    joined = jnp.einsum("...ij,...jk->...ik", left, right, precision=HIGH)
    scale = jnp.sum(joined, axis=(-2, -1)) / joined.shape[-1]
    return (joined / scale[..., None, None], left_log + right_log + jnp.log(scale))


def chain_product(mats, logs):
    while mats.shape[0] > 1:
        half = mats.shape[0] // 2
        joined, joined_log = chain_join(
            (mats[0 : 2 * half : 2], logs[0 : 2 * half : 2]),
            (mats[1 : 2 * half : 2], logs[1 : 2 * half : 2]),
        )
        mats, logs = (joined, joined_log)
    return (mats[0], logs[0])


def on_device(
    features,
    wear,
    rec_start,
    rec_end,
    conv_first,
    conv_second,
    emit_weight,
    leave,
    jump,
    init_logits,
    type_prior,
):
    persons = features.shape[1]
    span = features.shape[2]
    kinds = jump.shape[0]
    states = jump.shape[-1]
    tm_index = lax.axis_index("tm")
    type_index = lax.axis_index("type")
    total_epochs = span * lax.axis_size("tm")
    extended = padded(features, (("tm", 2),), 5)
    first = jnp.zeros((persons, span + 8, conv_first.shape[2]), jnp.float32)
    for tap in range(3):
        first = first + jnp.einsum(
            "ipt,ic->ptc",
            extended[:, :, tap : tap + span + 8],
            conv_first[tap],
            preferred_element_type=jnp.float32,
        )
    wide_pos = tm_index * span - 4 + jnp.arange(span + 8, dtype=jnp.int32)
    inside = (wide_pos >= 0) & (wide_pos < total_epochs)
    first = jnp.where(inside[None, :, None], jax.nn.silu(first), 0.0).astype(jnp.bfloat16)
    second = jnp.zeros((persons, span, conv_second.shape[2]), jnp.float32)
    for tap in range(3):
        second = second + jnp.einsum(
            "ptc,cd->ptd",
            first[:, 4 * tap : 4 * tap + span],
            conv_second[tap],
            preferred_element_type=jnp.float32,
        )
    second = jax.nn.silu(second).astype(jnp.bfloat16)
    logits = jnp.einsum("ptc,cm->ptm", second, emit_weight, preferred_element_type=jnp.float32)
    probs = jnp.exp(jax.nn.log_softmax(logits.reshape(persons, span, kinds, states), axis=-1))
    positions = tm_index * span + jnp.arange(span, dtype=jnp.int32)
    observed = (
        (wear > 0)
        & (positions[None, :] >= rec_start[:, None])
        & (positions[None, :] < rec_end[:, None])
    )
    emis = jnp.where(observed[:, :, None, None], probs, jnp.float32(1.0))
    observed_f = observed.astype(jnp.float32)
    eye_small = jnp.eye(states, dtype=jnp.float32)
    trans = (1.0 - leave)[..., None] * eye_small + leave[..., None] * jax.nn.softmax(jump, axis=-1)
    start = jax.nn.softmax(init_logits, axis=-1)
    start_all = jnp.broadcast_to(start, (persons, kinds, states))
    group = span // 16
    emis_blocks = jnp.transpose(emis.reshape(persons, 16, group, kinds, states), (1, 2, 0, 3, 4))
    eye_all = jnp.broadcast_to(eye_small, (persons, kinds, states, states))
    zero_logs = jnp.zeros((persons, kinds), jnp.float32)

    def block_leaves(block):
        return trans[None, None] * block[..., None, :]

    def pass_one(carry, block):
        leaves = block_leaves(block)
        product = chain_product(leaves, jnp.zeros(leaves.shape[:3], jnp.float32))
        return (chain_join(carry, product), None)

    (stretch, stretch_log), _ = lax.scan(pass_one, (eye_all, zero_logs), emis_blocks)
    before, before_log = prefix((stretch, stretch_log), "tm", chain_join, (eye_all, zero_logs))
    vec = jnp.einsum("pki,pkij->pkj", start_all, before, precision=HIGH)
    vec_total = jnp.sum(vec, axis=-1)
    alpha_in = vec / vec_total[..., None]
    log_in = before_log + jnp.log(vec_total)

    def advance(carry, inputs):
        alpha_now, log_now, occupied = carry
        emis_now, mask_now = inputs
        pred = jnp.einsum("pki,kij->pkj", alpha_now, trans, precision=HIGH)
        unnorm = pred * emis_now
        step_total = jnp.sum(unnorm, axis=-1)
        alpha_next = unnorm / step_total[..., None]
        occupied = occupied + mask_now[:, None, None] * alpha_next
        return ((alpha_next, log_now + jnp.log(step_total), occupied), alpha_next)

    zero_occupied = jnp.zeros((persons, kinds, states), jnp.float32)
    (alpha_end, own_log, occupied), history = lax.scan(
        advance,
        (alpha_in, zero_logs, zero_occupied),
        (jnp.transpose(emis, (1, 0, 2, 3)), observed_f.T),
    )
    filtered = jnp.transpose(history, (1, 0, 2, 3))
    contribution = log_in + own_log - log_in
    summed = lax.psum(contribution, "tm")
    full = lax.all_gather(summed, "type", axis=1, tiled=True)
    rate_full = full / total_epochs
    post_full = jax.nn.softmax(type_prior[None, :] + 8.0 * rate_full, axis=-1)
    offset = type_index * kinds
    rate_own = lax.dynamic_slice(rate_full, (jnp.int32(0), offset), (persons, kinds))
    post_own = lax.dynamic_slice(post_full, (jnp.int32(0), offset), (persons, kinds))
    numer = jnp.einsum("pk,pks->ks", post_own, occupied, precision=HIGH)
    denom = jnp.einsum("pk,p->k", post_own, jnp.sum(observed_f, axis=1), precision=HIGH)
    numer, denom = lax.psum((numer, denom), ("people", "tm"))
    occupancy = numer / denom[:, None]
    return (rate_own, post_own, occupancy, filtered)


def solution(mesh):
    return jax.shard_map(
        on_device,
        mesh=mesh,
        in_specs=(
            P(None, "people", "tm"),
            P("people", "tm"),
            P("people"),
            P("people"),
            P(),
            P(),
            P(None, "type"),
            P("type", None),
            P("type", None, None),
            P("type", None),
            P(),
        ),
        out_specs=(
            P("people", "type"),
            P("people", "type"),
            P("type", None),
            P("people", "tm", "type", None),
        ),
        check_vma=False,
    )
```

profile of v0, /device:TPU:1, one launch (start us, length us, event | category | flops | bytes accessed | tf_op | source)
XLA Modules:
  0.0 1187.6 jit_solution(14869745420775426021)
XLA Ops:
  8.0 4.6 collective-permute-start
  12.6 1.9 collective-permute-start.1
  15.9 1.3 convert_reduce_fusion
  18.1 1.5 fusion.37
  26.5 85.7 %while.46 = (s32[]{:T(128)}, f32[1,4,64,64]{2,3,1,0:T(8,128)S(1)}, f32[1,4]{1,0:T(1,128)S(1)}, f32[4,64,64]{2,1,0:T(8,128)S(1)}, f32[16,16,1,4,64]{4,3,1,2,0:T(4,128)S(1)}, /*index=5*/s32[]{:T(128)}, s32[]{:T(128)}) while((s32[]{:T(128)}, f32[1,4,64,64]{2,3,1,0:T(8,128)S(1)}, f32[1,4]{1,0:T(1,128)S(1)}, ...), condition=%wide.region_10.11_spmd.clone, body=%wide.region_4.0_spmd.clone.sunk | while | flops 202113104 | bytes 6277803 | solution.py:132
  26.8 1.4 fusion.97
  32.2 1.4 fusion.97
  37.5 1.4 fusion.97
  42.9 1.4 fusion.97
  48.3 1.4 fusion.97
  53.6 1.4 fusion.97
  59.0 1.4 fusion.97
  64.3 1.4 fusion.97
  69.7 1.4 fusion.97
  75.0 1.4 fusion.97
  80.4 1.4 fusion.97
  85.8 1.4 fusion.97
  91.1 1.4 fusion.97
  96.5 1.4 fusion.97
  101.8 1.4 fusion.97
  107.2 1.4 fusion.97
  115.0 43.8 %all-gather.2 = bf16[64,1,4]{2,1,0:T(2,128)(2,1)S(1)} all-gather(bf16[1,1,4]{2,1,0:T(2,128)(2,1)S(1)} %convert_bitcast_fusion.1), channel_id=3, replica_groups=mesh['people'=2,'tm'=64,'type'=2] {'tm'}, dimensions={0}, use_global_device_ids=true | all-gather | bytes 520 | tf_op jit(solution)/shard_map/all_gather | solution.py:25
  158.7 1.6 exponential_select_fusion
  160.4 36.0 %all-gather.5.cloned.1.call-done = bf16[64,4,64,64]{3,2,1,0:T(8,128)(2,1)} async-done(((bf16[1,4,64,64]{3,2,1,0:T(8,128)(2,1)}), bf16[64,4,64,64]{3,2,1,0:T(8,128)(2,1)}) %all-gather.5.cloned.1.call-update) | async-done | bytes 2097168 | tf_op jit(solution)/shard_map/all_gather | solution.py:25
  196.4 86.0 %while.47 = (s32[]{:T(128)}, f32[1,4,64,64]{2,3,1,0:T(8,128)S(1)}, f32[1,4]{1,0:T(1,128)S(1)}, s32[]{:T(128)}, bf16[64,1,4,64,64]{4,3,2,0,1:T(8,128)(2,1)}, /*in...) while((s32[]{:T(128)}, f32[1,4,64,64]{2,3,1,0:T(8,128)S(1)}, f32[1,4]{1,0:T(1,128)S(1)}, ...), condition=%wide.region_13.14_spmd.clone, body=%wide.region_11.13_spmd.clone.sunk | while | flops 12632092 | bytes 393958 | solution.py:42
  199.1 1.2 fusion.104
  201.8 1.2 fusion.104
  205.8 1.2 fusion.104
  208.5 1.2 fusion.104
  212.6 1.2 fusion.104
  215.2 1.2 fusion.104
  219.3 1.2 fusion.104
  222.0 1.2 fusion.104
  226.0 1.2 fusion.104
  228.7 1.2 fusion.104
  232.7 1.2 fusion.104
  239.4 1.2 fusion.104
  246.2 1.2 fusion.104
  252.9 1.2 fusion.104
  259.6 1.2 fusion.104
  266.3 1.2 fusion.104
  273.0 1.2 fusion.104
  279.8 1.2 fusion.104
  282.9 438.0 %while.48 = (s32[]{:T(128)}, f32[1,4,64]{2,1,0:T(4,128)S(1)}, f32[1,4]{1,0:T(1,128)S(1)}, f32[1,4,64]{2,1,0:T(4,128)S(1)}, f32[256,1,4,64]{3,2,1,0:T(4,128)S(1)}...) while((s32[]{:T(128)}, f32[1,4,64]{2,1,0:T(4,128)S(1)}, ...), condition=%wide.region_19.20_spmd.clone, body=%wide.region_17.19_spmd.clone.sunk | while | flops 198407 | bytes 81608 | solution.py:150
  721.0 123.7 %psum.21 = f32[1,4]{1,0:T(1,128)S(1)} all-reduce(f32[1,4]{1,0:T(1,128)S(1)} %add_subtract_fusion), channel_id=1, replica_groups=mesh['people'=2,'tm'=64,'type'=2] {'tm'}, use_global_device_ids=true, to_apply=%region_20.21 | all-reduce | flops 4 | bytes 32 | tf_op jit(solution)/shard_map/psum | solution.py:157
  845.7 3.8 all-reduce
  850.0 1.3 fusion.68
  853.3 326.8 %all-reduce.1 = (f32[4,64]{1,0:T(4,128)S(1)}, f32[4]{0:T(128)S(1)}) all-reduce(f32[4,64]{1,0:T(4,128)S(1)} %bitcast_multiply_fusion.1, f32[4]{0:T(128)S(1)} %get-tuple-element.317), channel_id=1, replica_groups=mesh['people'=2,'tm'=64,'type'=2] {'people','tm'}, use_global_device_ids=true, to_apply=%region_23.24 | all-reduce | flops 260 | bytes 2080 | tf_op jit(solution)/shard_map/psum | solution.py:166
  (2270 shorter events, 572.2 us)
Async XLA Ops:
  7.2 17.2 %copy-start = (bf16[128,256]{1,0:T(8,128)(2,1)S(1)}, bf16[128,256]{1,0:T(8,128)(2,1)}, u32[]{:S(2)}) copy-start(bf16[128,256]{1,0:T(8,128)(2,1)} %param.23) | copy-start | bytes 196612
  7.2 17.0 %copy-start.1 = (bf16[3,128,128]{2,1,0:T(8,128)(2,1)S(1)}, bf16[3,128,128]{2,1,0:T(8,128)(2,1)}, u32[]{:S(2)}) copy-start(bf16[3,128,128]{2,1,0:T(8,128)(2,1)} %param.22) | copy-start | bytes 294916
  7.2 189.2 %all-gather.5.cloned.1.call-start = ((), (), s32[]{:S(2)}) async-start(), calls=%async_computation | async-start | bytes 4259840 | tf_op jit(solution)/shard_map/all_gather | solution.py:25
  8.0 11.6 collective-permute-start
  12.6 7.0 collective-permute-start.1
  26.5 86.6 %copy-start.2 = (f32[4,64]{1,0:T(4,128)S(1)}, f32[4,64]{1,0:T(4,128)}, u32[]{:S(2)}) copy-start(f32[4,64]{1,0:T(4,128)} %param.26) | copy-start | bytes 3076
  26.5 86.7 %copy-start.5 = (u32[256]{0:T(256)S(1)}, u32[256]{0:T(256)}, u32[]{:S(2)}) copy-start(u32[256]{0:T(256)} %constant.125) | copy-start | bytes 3076
  196.4 653.0 %copy-start.4 = (f32[8]{0:T(128)S(1)}, f32[8]{0:T(128)}, u32[]{:S(2)}) copy-start(f32[8]{0:T(128)} %param.27) | copy-start | bytes 100
  853.2 327.5 %copy-start.3 = (f32[1,4]{1,0:T(1,128)}, f32[1,4]{1,0:T(1,128)S(1)}, u32[]{:S(2)}) copy-start(f32[1,4]{1,0:T(1,128)S(1)} %get-tuple-element.318) | copy-start | bytes 52
Sparse Core Ops, SparseCore 0:
  113.1 83.2 all-gather.4
where the time goes:
time: 1190 us
  blocking collectives  498 us (42%)
  other arithmetic  258 us (22%)
  matrix products  195 us (16%)
  local copies, waits for them, and re-layouts  168 us (14%)
  waiting for transfers between devices  36 us (3%)
  between operations  16.3 us (1%)
    psum x1, blocking collectives, on_device(): numer, denom = lax.psum((numer, denom), ('people', 'tm'))  327 us
    add x256, other arithmetic, advance(): occupied = occupied + mask_now[:, None, None] * alpha_next  168 us
    dynamic_slice x256, local copies, waits for them, and re-layouts, on_device(): lax.scan(advance, (alpha_in, zero_logs, zero_occupied), (jnp.transpose(em...  151 us
    dot_general x144, matrix products, chain_join(): joined = jnp.einsum('...ij,...jk->...ik', left, right, precision=HIGH)  134 us
    psum x1, blocking collectives, on_device(): summed = lax.psum(contribution, 'tm')  124 us
    dot_general x256, matrix products, advance(): pred = jnp.einsum('pki,kij->pkj', alpha_now, trans, precision=HIGH)  57.1 us
    all_gather x1, blocking collectives, prefix(): lax.all_gather(part.astype(kind), axis)  43.8 us
    all_gather x1, waiting for transfers between devices, prefix(): lax.all_gather(part.astype(kind), axis)  36 us
  transfers between devices with their start and end apart: 3, of which 1 were waited for; matrix products, arithmetic and copies ran while one was open for 1% of the time, Pallas kernels for 0%

commit v1 on v0

--- a/solution.py
+++ b/solution.py
@@ -2,6 +2,7 @@
 import jax.numpy as jnp
 from jax import lax
 from jax.sharding import PartitionSpec as P
+from jax.lax import all_gather
 
 HIGH = lax.Precision.HIGHEST
 
@@ -154,7 +155,7 @@
     )
     filtered = jnp.transpose(history, (1, 0, 2, 3))
     contribution = log_in + own_log - log_in
-    summed = lax.psum(contribution, "tm")
+    summed = jnp.sum(all_gather(contribution, "tm"), 0)
     full = lax.all_gather(summed, "type", axis=1, tiled=True)
     rate_full = full / total_epochs
     post_full = jax.nn.softmax(type_prior[None, :] + 8.0 * rate_full, axis=-1)

time: 1190 us -> 1110 us (0.933)
  blocking collectives: 498 us -> 409 us
    psum x1 -> x0, blocking collectives: 124 us -> none  [on_device(): summed = lax.psum(contribution, 'tm')]
    all_gather x0 -> x1, blocking collectives: none -> 37.5 us  [on_device(): summed = jnp.sum(all_gather(contribution, 'tm'), 0)]
where the time goes in v1:
time: 1110 us; the launch traced here: 1100 us
  blocking collectives  409 us (37%)
  other arithmetic  258 us (23%)
  matrix products  195 us (18%)
  local copies, waits for them, and re-layouts  168 us (15%)
  waiting for transfers between devices  36 us (3%)
  between operations  16.3 us (1%)
    psum x1, blocking collectives, on_device(): numer, denom = lax.psum((numer, denom), ('people', 'tm'))  324 us
    add x256, other arithmetic, advance(): occupied = occupied + mask_now[:, None, None] * alpha_next  168 us
    dynamic_slice x256, local copies, waits for them, and re-layouts, on_device(): lax.scan(advance, (alpha_in, zero_logs, zero_occupied), (jnp.transpose(em...  151 us
    dot_general x144, matrix products, chain_join(): joined = jnp.einsum('...ij,...jk->...ik', left, right, precision=HIGH)  134 us
    dot_general x256, matrix products, advance(): pred = jnp.einsum('pki,kij->pkj', alpha_now, trans, precision=HIGH)  57.1 us
    all_gather x1, blocking collectives, prefix(): lax.all_gather(part.astype(kind), axis)  43.8 us
    all_gather x1, blocking collectives, on_device(): summed = jnp.sum(all_gather(contribution, 'tm'), 0)  37.5 us
    all_gather x1, waiting for transfers between devices, prefix(): lax.all_gather(part.astype(kind), axis)  36 us
  transfers between devices with their start and end apart: 3, of which 1 were waited for; matrix products, arithmetic and copies ran while one was open for 1% of the time, Pallas kernels for 0%

profile of v1, /device:TPU:1, one launch (start us, length us, event | category | flops | bytes accessed | tf_op | source)
XLA Modules:
  0.0 1099.2 jit_solution(9225135185024129812)
XLA Ops:
  8.0 4.6 collective-permute-start
  12.6 1.9 collective-permute-start.1
  15.9 1.3 convert_reduce_fusion
  18.1 1.5 fusion.37
  26.5 85.7 %while.46 = (s32[]{:T(128)}, f32[1,4,64,64]{2,3,1,0:T(8,128)S(1)}, f32[1,4]{1,0:T(1,128)S(1)}, f32[4,64,64]{2,1,0:T(8,128)S(1)}, f32[16,16,1,4,64]{4,3,1,2,0:T(4,128)S(1)}, /*index=5*/s32[]{:T(128)}, s32[]{:T(128)}) while((s32[]{:T(128)}, f32[1,4,64,64]{2,3,1,0:T(8,128)S(1)}, f32[1,4]{1,0:T(1,128)S(1)}, ...), condition=%wide.region_10.11_spmd.clone, body=%wide.region_4.0_spmd.clone.sunk | while | flops 202113104 | bytes 6277803 | solution.py:133
  26.8 1.4 fusion.98
  32.2 1.4 fusion.98
  37.5 1.4 fusion.98
  42.9 1.4 fusion.98
  48.3 1.4 fusion.98
  53.6 1.4 fusion.98
  59.0 1.4 fusion.98
  64.3 1.4 fusion.98
  69.7 1.4 fusion.98
  75.0 1.4 fusion.98
  80.4 1.4 fusion.98
  85.8 1.4 fusion.98
  91.1 1.4 fusion.98
  96.5 1.4 fusion.98
  101.8 1.4 fusion.98
  107.2 1.4 fusion.98
  114.9 43.8 %all-gather.4 = bf16[64,1,4]{2,1,0:T(2,128)(2,1)S(1)} all-gather(bf16[1,1,4]{2,1,0:T(2,128)(2,1)S(1)} %convert_bitcast_fusion.1), channel_id=3, replica_groups=mesh['people'=2,'tm'=64,'type'=2] {'tm'}, dimensions={0}, use_global_device_ids=true | all-gather | bytes 520 | tf_op jit(solution)/shard_map/all_gather | solution.py:26
  158.7 1.6 exponential_select_fusion
  160.4 36.0 %all-gather.8.cloned.1.call-done = bf16[64,4,64,64]{3,2,1,0:T(8,128)(2,1)} async-done(((bf16[1,4,64,64]{3,2,1,0:T(8,128)(2,1)}), bf16[64,4,64,64]{3,2,1,0:T(8,128)(2,1)}) %all-gather.8.cloned.1.call-update) | async-done | bytes 2097168 | tf_op jit(solution)/shard_map/all_gather | solution.py:26
  196.4 86.0 %while.47 = (s32[]{:T(128)}, f32[1,4,64,64]{2,3,1,0:T(8,128)S(1)}, f32[1,4]{1,0:T(1,128)S(1)}, s32[]{:T(128)}, bf16[64,1,4,64,64]{4,3,2,0,1:T(8,128)(2,1)}, /*in...) while((s32[]{:T(128)}, f32[1,4,64,64]{2,3,1,0:T(8,128)S(1)}, f32[1,4]{1,0:T(1,128)S(1)}, ...), condition=%wide.region_13.14_spmd.clone, body=%wide.region_11.13_spmd.clone.sunk | while | flops 12632092 | bytes 393958 | solution.py:43
  199.1 1.2 fusion.105
  203.1 1.2 fusion.105
  205.8 1.2 fusion.105
  209.9 1.2 fusion.105
  212.5 1.2 fusion.105
  216.6 1.2 fusion.105
  219.3 1.2 fusion.105
  223.3 1.2 fusion.105
  226.0 1.2 fusion.105
  230.0 1.2 fusion.105
  232.7 1.2 fusion.105
  236.7 1.2 fusion.105
  243.5 1.2 fusion.105
  250.2 1.2 fusion.105
  256.9 1.2 fusion.105
  263.6 1.2 fusion.105
  270.3 1.2 fusion.105
  277.1 1.2 fusion.105
  282.9 438.0 %while.48 = (s32[]{:T(128)}, f32[1,4,64]{2,1,0:T(4,128)S(1)}, f32[1,4]{1,0:T(1,128)S(1)}, f32[1,4,64]{2,1,0:T(4,128)S(1)}, f32[256,1,4,64]{3,2,1,0:T(4,128)S(1)}...) while((s32[]{:T(128)}, f32[1,4,64]{2,1,0:T(4,128)S(1)}, ...), condition=%wide.region_19.20_spmd.clone, body=%wide.region_17.19_spmd.clone.sunk | while | flops 198407 | bytes 81608 | solution.py:151
  721.0 37.5 %all-gather.5 = f32[64,1,4]{2,1,0:T(1,128)S(1)} all-gather(f32[1,1,4]{2,1,0:T(1,128)S(1)} %fusion.65), channel_id=4, replica_groups=mesh['people'=2,'tm'=64,'type'=2] {'tm'}, dimensions={0}, use_global_device_ids=true | all-gather | bytes 1040 | tf_op jit(solution)/shard_map/all_gather | solution.py:158
  759.7 3.8 all-reduce
  764.1 1.3 fusion.69
  767.4 324.4 %all-reduce.1 = (f32[4,64]{1,0:T(4,128)S(1)}, f32[4]{0:T(128)S(1)}) all-reduce(f32[4,64]{1,0:T(4,128)S(1)} %bitcast_multiply_fusion.1, f32[4]{0:T(128)S(1)} %get-tuple-element.317), channel_id=1, replica_groups=mesh['people'=2,'tm'=64,'type'=2] {'people','tm'}, use_global_device_ids=true, to_apply=%region_23.24 | all-reduce | flops 260 | bytes 2080 | tf_op jit(solution)/shard_map/psum | solution.py:167
  (2271 shorter events, 572.5 us)
Async XLA Ops:
  7.2 17.2 %copy-start = (bf16[128,256]{1,0:T(8,128)(2,1)S(1)}, bf16[128,256]{1,0:T(8,128)(2,1)}, u32[]{:S(2)}) copy-start(bf16[128,256]{1,0:T(8,128)(2,1)} %param.23) | copy-start | bytes 196612
  7.2 17.0 %copy-start.1 = (bf16[3,128,128]{2,1,0:T(8,128)(2,1)S(1)}, bf16[3,128,128]{2,1,0:T(8,128)(2,1)}, u32[]{:S(2)}) copy-start(bf16[3,128,128]{2,1,0:T(8,128)(2,1)} %param.22) | copy-start | bytes 294916
  7.2 189.2 %all-gather.8.cloned.1.call-start = ((), (), s32[]{:S(2)}) async-start(), calls=%async_computation | async-start | bytes 4259840 | tf_op jit(solution)/shard_map/all_gather | solution.py:26
  8.0 11.6 %collective-permute-start = (bf16[3,1,5]{2,0,1:T(4,128)(2,1)S(1)}, bf16[3,1,5]{2,0,1:T(4,128)(2,1)S(1)}, u32[]{:S(2)}, u32[]{:S(2)}) collective-permute-start(bf16[3,1,5]{2,0,1:T(4,128)(2,1)S(1)} %get-tuple-element.343), channel_id=1, source_target_pairs={{0,2},{2,4},{4,6},{6,8},{8,10},{10,12},{12,14},{14,16},{16,18},{18... | collective-permute-start | bytes 98 | tf_op jit(solution)/shard_map/ppermute | solution.py:15
  12.6 7.0 collective-permute-start.1
  26.5 86.6 %copy-start.2 = (f32[4,64]{1,0:T(4,128)S(1)}, f32[4,64]{1,0:T(4,128)}, u32[]{:S(2)}) copy-start(f32[4,64]{1,0:T(4,128)} %param.26) | copy-start | bytes 3076
  26.5 86.7 %copy-start.5 = (u32[256]{0:T(256)S(1)}, u32[256]{0:T(256)}, u32[]{:S(2)}) copy-start(u32[256]{0:T(256)} %constant.125) | copy-start | bytes 3076
  196.4 567.1 %copy-start.4 = (f32[8]{0:T(128)S(1)}, f32[8]{0:T(128)}, u32[]{:S(2)}) copy-start(f32[8]{0:T(128)} %param.27) | copy-start | bytes 100
  767.3 325.1 %copy-start.3 = (f32[4]{0:T(128)}, f32[4]{0:T(128)S(1)}, u32[]{:S(2)}) copy-start(f32[4]{0:T(128)S(1)} %get-tuple-element.318) | copy-start | bytes 52
Sparse Core Ops, SparseCore 0:
  113.1 83.2 all-gather.7
